TPU v7x, 128 devices: a whole 4x4x4 slice. The times are simulated.
128 devices in a mesh: band: 32 (over z, x, core), seg: 4 (over y).
Axes of the slice: x: 4, y: 4, z: 4, core: 2. Of those that a mesh axis runs over, the one named last changes fastest.
Arguments:
- voltages: float32 [4, 1, 2, 2, 1024, 3072], P('seg', None, None, None, 'band'), may hold values from -6 to 6
- chirp_phase: float32 [1, 1024, 4096], P(None, 'seg', 'band'), may hold values from -3.140625 to 3.140625
Outputs:
- dedispersed: float32 [4, 1, 2, 2, 1024, 3072], P('seg', None, None, None, 'band')
All inputs are finite; a program needn't handle non-finite values.
Results may differ from a plain program's by a relative error of at most 0.00015.
Values sent between devices are 32-bit elements; how exact they have to be, the bound alone decides.
No kernel may reach another device: no remote copies, remote signals or barrier semaphores. Data moves between devices by JAX's collectives and lax.ppermute only.
A program may use at most 64 MiB of HBM per device.

v0:
```python
import math
import jax
import jax.numpy as jnp
from jax import lax
from jax.sharding import PartitionSpec as P


def passed_along(block, axis, distance):
    devices = range(lax.axis_size(axis))
    route = [(i - distance, i) for i in devices if i - distance in devices]
    return lax.ppermute(block, axis, route)


def gathered(block, axis, dim):
    size = lax.axis_size(axis)
    pieces = [block]
    for shift in range(1, size):
        route = [((i + shift) % size, i) for i in range(size)]
        pieces.append(lax.ppermute(block, axis, route))
    ahead = jnp.stack(pieces, axis=0)
    ordered = jnp.roll(ahead, lax.axis_index(axis), axis=0)
    ordered = jnp.moveaxis(ordered, 0, dim)
    shape = list(block.shape)
    shape[dim] *= size
    return ordered.reshape(shape)


def split_factor(length):
    factor = int(math.isqrt(length))
    while length % factor:
        factor -= 1
    return factor


def tables(length, direction):
    places = jnp.arange(length, dtype=jnp.int32)
    product = places[:, None] * places[None, :] % length
    angles = direction * 2.0 * math.pi / length * product.astype(jnp.float32)
    return (jnp.cos(angles), jnp.sin(angles))


def rotate(real_part, imag_part, product, scale):
    angles = scale * product.astype(jnp.float32)
    cosine = jnp.cos(angles)
    sine = jnp.sin(angles)
    return (real_part * cosine - imag_part * sine, real_part * sine + imag_part * cosine)


def transform_last(real_part, imag_part, direction):
    length = real_part.shape[-1]
    inner = split_factor(length)
    outer = length // inner
    leading = real_part.shape[:-1]
    real_part = real_part.reshape(leading + (outer, inner))
    imag_part = imag_part.reshape(leading + (outer, inner))
    cos_outer, sin_outer = tables(outer, direction)
    highest = lax.Precision.HIGHEST
    first_real = jnp.einsum(
        "...nj,nk->...kj", real_part, cos_outer, precision=highest
    ) - jnp.einsum("...nj,nk->...kj", imag_part, sin_outer, precision=highest)
    first_imag = jnp.einsum(
        "...nj,nk->...kj", real_part, sin_outer, precision=highest
    ) + jnp.einsum("...nj,nk->...kj", imag_part, cos_outer, precision=highest)
    outer_index = jnp.arange(outer, dtype=jnp.int32)[:, None]
    inner_index = jnp.arange(inner, dtype=jnp.int32)[None, :]
    first_real, first_imag = rotate(
        first_real,
        first_imag,
        outer_index * inner_index % length,
        direction * 2.0 * math.pi / length,
    )
    cos_inner, sin_inner = tables(inner, direction)
    last_real = jnp.matmul(first_real, cos_inner, precision=highest) - jnp.matmul(
        first_imag, sin_inner, precision=highest
    )
    last_imag = jnp.matmul(first_real, sin_inner, precision=highest) + jnp.matmul(
        first_imag, cos_inner, precision=highest
    )
    last_real = jnp.swapaxes(last_real, -1, -2).reshape(leading + (length,))
    last_imag = jnp.swapaxes(last_imag, -1, -2).reshape(leading + (length,))
    return (last_real, last_imag)


def transform_rows(real_part, imag_part, direction):
    result_real, result_imag = transform_last(
        jnp.swapaxes(real_part, -1, -2), jnp.swapaxes(imag_part, -1, -2), direction
    )
    return (jnp.swapaxes(result_real, -1, -2), jnp.swapaxes(result_imag, -1, -2))


def row_pass(spread):
    result_real, result_imag = transform_rows(spread[:, :, 0], spread[:, :, 1], -1.0)
    return jnp.stack([result_real, result_imag], axis=2)


def column_pass(gathered):
    cols = gathered.shape[-1]
    length_scale = 1.0 / (gathered.shape[-2] * lax.axis_size("band") * cols)
    result_real, result_imag = transform_last(gathered[:, :, 0], gathered[:, :, 1], 1.0)
    result = jnp.stack([result_real * length_scale, result_imag * length_scale], axis=2)
    return result[..., cols // 4 :]


def per_device(voltages, chirp_phase):
    block = voltages[0]
    rows_dev = block.shape[3]
    valid_cols = block.shape[4]
    cols = valid_cols * 4 // 3
    bands = lax.axis_size("band")
    rows = rows_dev * bands
    length = rows * cols
    width = cols // bands
    tail = block[..., valid_cols - cols // 4 :]
    history = passed_along(tail, "seg", 1)
    buffer = jnp.concatenate([history, block], axis=-1)
    real_part, imag_part = transform_last(buffer[:, :, 0], buffer[:, :, 1], -1.0)
    row_index = lax.axis_index("band") * rows_dev + jnp.arange(rows_dev, dtype=jnp.int32)
    col_index = jnp.arange(cols, dtype=jnp.int32)
    real_part, imag_part = rotate(
        real_part,
        imag_part,
        row_index[:, None] * col_index[None, :] % length,
        -2.0 * math.pi / length,
    )
    stacked = jnp.stack([real_part, imag_part], axis=2)
    spectra = row_pass(lax.all_to_all(stacked, "band", split_axis=4, concat_axis=3, tiled=True))
    real_part, imag_part = (spectra[:, :, 0], spectra[:, :, 1])
    phases = gathered(chirp_phase, "seg", 1)
    cosine = jnp.cos(phases)[:, None]
    sine = jnp.sin(phases)[:, None]
    real_part, imag_part = (
        real_part * cosine - imag_part * sine,
        real_part * sine + imag_part * cosine,
    )
    real_part, imag_part = transform_rows(real_part, imag_part, 1.0)
    full_rows = jnp.arange(rows, dtype=jnp.int32)
    own_cols = lax.axis_index("band") * width + jnp.arange(width, dtype=jnp.int32)
    real_part, imag_part = rotate(
        real_part,
        imag_part,
        full_rows[:, None] * own_cols[None, :] % length,
        2.0 * math.pi / length,
    )
    columns = jnp.stack([real_part, imag_part], axis=2)
    result = column_pass(lax.all_to_all(columns, "band", split_axis=3, concat_axis=4, tiled=True))
    return result[None]


def solution(mesh):
    in_specs = (P("seg", None, None, None, "band", None), P(None, "seg", "band"))
    out_specs = P("seg", None, None, None, "band", None)
    return jax.shard_map(
        per_device, mesh=mesh, in_specs=in_specs, out_specs=out_specs, check_vma=False
    )
```

profile of v0, /device:TPU:8, one launch (start us, length us, event | category | flops | bytes accessed | tf_op | source)
XLA Modules:
  0.0 270.5 jit_solution(694913317675415932)
XLA Ops:
  8.0 3.3 %fusion.81 = (f32[32,4096]{1,0:T(8,128)}, f32[32,4096]{1,0:T(8,128)}) fusion(s32[32]{0:T(128)S(1)} %iota_add_fusion.1), kind=kLoop, calls=%fused_computation.117 | loop fusion | flops 1835008 | bytes 1048704 | tf_op jit(solution)/shard_map/cos | solution.py:44
  14.3 7.1 %collective-permute-done = f32[1,2,2,32,1024]{4,3,2,1,0:T(8,128)} collective-permute-done((f32[1,2,2,32,1024]{4,3,2,1,0:T(8,128)S(1)}, f32[1,2,2,32,1024]{4,3,2,1,0:T(8,128)}, u32[]{:S(2)}, u32[]{:S(2)}) %collective-permute-start) | collective-permute-done | bytes 524320 | tf_op jit(solution)/shard_map/ppermute | solution.py:11
  26.1 3.3 %fusion.92 = f32[64,2,32,64]{3,0,2,1:T(8,128)} fusion(f32[2,32,64,64]{3,2,1,0:T(8,128)S(1)} %reshape.541), kind=kOutput, calls=%fused_computation.141 | convolution fusion | flops 201383936 | bytes 2097152 | tf_op jit(solution)/shard_map/...nj,nk->...kj/dot_general | solution.py:60
  29.4 3.4 %fusion.96 = f32[64,2,32,64]{3,0,2,1:T(8,128)} fusion(f32[2,32,64,64]{3,2,1,0:T(8,128)S(1)} %reshape.541), kind=kOutput, calls=%fused_computation.145 | convolution fusion | flops 201383936 | bytes 2097152 | tf_op jit(solution)/shard_map/...nj,nk->...kj/dot_general | solution.py:63
  35.0 4.4 %convolution_subtract_fusion.1 = f32[64,2,32,64]{3,0,2,1:T(8,128)S(1)} fusion(f32[64,2,32,64]{3,0,2,1:T(8,128)} %fusion.92, f32[2,32,64,64]{3,2,1,0:T(8,128)} %reshape.540), kind=kOutput, calls=%fused_computation.39 | convolution fusion | flops 201646080 | bytes 3145728 | tf_op jit(solution)/shard_map/...nj,nk->...kj/dot_general | solution.py:58
  43.6 3.5 %fusion.10 = f32[2,32,64,64]{3,2,1,0:T(8,128)} fusion(f32[64,2,32,64]{3,0,2,1:T(8,128)S(1)} %convolution_add_fusion.1, f32[64,2,32,64]{3,0,2,1:T(8,128)S(1)} %convolution_subtract_fusion.1, f32[64,64]{1,0:T(8,128)S(1)} %get-tuple-element.25, f32[64,64]{1,0:T(8,128)S(1)} %get-tuple-element.26), kind=kOutput, calls=%fused_computation.18 | convolution fusion | flops 202170368 | bytes 3178496 | tf_op jit(solution)/shard_map/dot_general | solution.py:76
  47.1 3.4 %subtract_bitcast_fusion = f32[1,2,32,64,64]{3,4,2,1,0:T(8,128)} fusion(f32[2,32,64,64]{3,2,1,0:T(8,128)S(1)} %fusion.12, f32[64,2,32,64]{3,0,2,1:T(8,128)S(1)} %convolution_add_fusion.1, f32[64,2,32,64]{3,0,2,1:T(8,128)S(1)} %convolution_subtract_fusion.1, f32[64,64]{1,0:T(8,128)S(1)} %get-tuple-element.25, f32[64,64]{1,0:T(8,128)S(1)} %get-tuple-element.26), kind=kOutput, calls=%fused_computation.35 | convolution fusion | flops 202432512 | bytes 4227072 | tf_op jit(solution)/shard_map/dot_general | solution.py:73
  55.6 5.5 %add_bitcast_fusion = f32[1,2,32,64,64]{3,4,2,1,0:T(8,128)} fusion(f32[2,32,64,64]{3,2,1,0:T(8,128)} %fusion.10, f32[64,2,32,64]{3,0,2,1:T(8,128)} %copy-done, f32[64,2,32,64]{3,0,2,1:T(8,128)S(1)} %convolution_subtract_fusion.1, f32[64,64]{1,0:T(8,128)S(1)} %get-tuple-element.25, f32[64,64]{1,0:T(8,128)S(1)} %get-tuple-element.26), kind=kOutput, calls=%fused_computation.34 | convolution fusion | flops 202432512 | bytes 4227072 | tf_op jit(solution)/shard_map/dot_general | solution.py:76
  66.6 8.4 %copy.121 = f32[1,2,2,32,4096]{3,1,2,0,4:T(2,128)} copy(f32[1,2,2,32,4096]{4,3,1,2,0:T(8,128)S(1)} %pad_maximum_fusion) | data formatting | bytes 4194304 | tf_op jit(solution)/shard_map/stack | solution.py:125
  75.0 10.9 %reshape.578 = f32[32,1,16384]{2,1,0:T(1,128)} reshape(f32[4096,1,2,2,32]{4,3,2,1,0:T(2,128)} %bitcast.361) | data formatting | bytes 4194304
  85.8 8.5 %all-to-all-start = ((f32[32,1,16384]{2,1,0:T(1,128)}), f32[32,1,16384]{2,1,0:T(1,128)S(1)}, u32[]{:S(2)}, u32[]{:S(2)}) async-start(f32[32,1,16384]{2,1,0:T(1,128)} %reshape.578), calls=%async_computation | async-start | bytes 4194304 | tf_op jit(solution)/shard_map/all_to_all | solution.py:126
  105.1 19.2 %all-to-all-done = f32[32,1,16384]{2,1,0:T(1,128)S(1)} async-done(((f32[32,1,16384]{2,1,0:T(1,128)}), f32[32,1,16384]{2,1,0:T(1,128)S(1)}, u32[]{:S(2)}, u32[]{:S(2)}) %all-to-all-start) | async-done | bytes 2097184 | tf_op jit(solution)/shard_map/all_to_all | solution.py:126
  126.2 7.4 %reduce.4 = f32[32,16384]{1,0:T(8,128)S(1)} reduce(f32[32,1,16384]{2,1,0:T(1,128)} %copy-done.6, f32[]{:T(128)} %broadcast.762), dimensions={1}, to_apply=%all_to_all.26.reduce_sub_computation | reduce | bytes 4194308 | tf_op jit(solution)/shard_map/all_to_all | solution.py:126
  133.6 8.5 %reshape.579 = f32[4096,1,2,2,32]{4,3,2,1,0:T(2,128)} reshape(f32[32,16384]{1,0:T(8,128)S(1)} %reduce.4) | data formatting | bytes 4194304
  142.1 10.8 %copy.122 = f32[1,2,2,32,4096]{4,0,3,2,1:T(1,128)S(1)} copy(f32[1,2,2,32,4096]{3,1,2,0,4:T(2,128)} %bitcast.362) | data formatting | bytes 4194304 | tf_op jit(solution)/shard_map/all_to_all | solution.py:126
  185.0 4.0 %all-to-all-start.1 = ((f32[1,2,2,1024,128]{4,1,2,0,3:T(2,128)}), f32[1,2,2,1024,128]{4,1,2,0,3:T(2,128)S(1)}, u32[]{:S(2)}, u32[]{:S(2)}) async-start(f32[1,2,2,1024,128]{4,1,2,0,3:T(2,128)} %copy.140), calls=%async_computation.1 | async-start | bytes 4194304 | tf_op jit(solution)/shard_map/all_to_all | solution.py:145
  189.2 29.8 %all-to-all-done.1 = f32[1,2,2,1024,128]{4,1,2,0,3:T(2,128)S(1)} async-done(((f32[1,2,2,1024,128]{4,1,2,0,3:T(2,128)}), f32[1,2,2,1024,128]{4,1,2,0,3:T(2,128)S(1)}, u32[]{:S(2)}, u32[]{:S(2)}) %all-to-all-start.1) | async-done | bytes 2097184 | tf_op jit(solution)/shard_map/all_to_all | solution.py:145
  220.4 6.4 %slice_reduce_fusion = (f32[2,32,4096]{2,1,0:T(8,128)S(1)}, f32[2,32,4096]{2,1,0:T(8,128)}) fusion(f32[1,2,2,32,4096]{4,0,3,2,1:T(1,128)S(1)} %bitcast.369), kind=kLoop, calls=%fused_computation.59 | loop fusion | bytes 4194304 | tf_op jit(solution)/shard_map/slice | solution.py:99
  229.2 3.3 %fusion.102 = f32[64,2,32,64]{3,0,2,1:T(8,128)} fusion(f32[2,32,64,64]{3,2,1,0:T(8,128)S(1)} %reshape.556), kind=kOutput, calls=%fused_computation.151 | convolution fusion | flops 201383936 | bytes 2097152 | tf_op jit(solution)/shard_map/...nj,nk->...kj/dot_general | solution.py:58
  232.5 3.4 %fusion.86 = f32[64,2,32,64]{3,0,2,1:T(8,128)} fusion(f32[2,32,64,64]{3,2,1,0:T(8,128)S(1)} %reshape.556), kind=kOutput, calls=%fused_computation.135 | convolution fusion | flops 201383936 | bytes 2097152 | tf_op jit(solution)/shard_map/...nj,nk->...kj/dot_general | solution.py:61
  238.1 4.4 %convolution_subtract_fusion = f32[64,2,32,64]{3,0,2,1:T(8,128)S(1)} fusion(f32[64,2,32,64]{3,0,2,1:T(8,128)} %fusion.102, f32[2,32,64,64]{3,2,1,0:T(8,128)} %reshape.557), kind=kOutput, calls=%fused_computation.37 | convolution fusion | flops 201646080 | bytes 3145728 | tf_op jit(solution)/shard_map/...nj,nk->...kj/dot_general | solution.py:60
  246.7 3.5 %fusion = f32[2,32,64,64]{3,2,1,0:T(8,128)} fusion(f32[64,2,32,64]{3,0,2,1:T(8,128)S(1)} %convolution_add_fusion, f32[64,2,32,64]{3,0,2,1:T(8,128)S(1)} %convolution_subtract_fusion, f32[64,64]{1,0:T(8,128)S(1)} %get-tuple-element.31, f32[64,64]{1,0:T(8,128)S(1)} %get-tuple-element.32), kind=kOutput, calls=%fused_computation.4 | convolution fusion | flops 202170368 | bytes 3178496 | tf_op jit(solution)/shard_map/dot_general | solution.py:76
  250.2 3.4 %multiply_bitcast_fusion.1 = f32[1,2,32,64,64]{3,4,2,1,0:T(8,128)} fusion(f32[2,32,64,64]{3,2,1,0:T(8,128)S(1)} %fusion.2, f32[64,2,32,64]{3,0,2,1:T(8,128)S(1)} %convolution_add_fusion, f32[64,2,32,64]{3,0,2,1:T(8,128)S(1)} %convolution_subtract_fusion, f32[64,64]{1,0:T(8,128)S(1)} %get-tuple-element.31, f32[64,64]{1,0:T(8,128)S(1)} %get-tuple-element.32), kind=kOutput, calls=%fused_computation.33 | convolution fusion | flops 202694656 | bytes 4227072 | tf_op jit(solution)/shard_map/dot_general | solution.py:73
  258.7 5.5 %multiply_bitcast_fusion = f32[1,2,32,64,64]{3,4,2,1,0:T(8,128)} fusion(f32[2,32,64,64]{3,2,1,0:T(8,128)} %fusion, f32[64,2,32,64]{3,0,2,1:T(8,128)} %copy-done.1, f32[64,2,32,64]{3,0,2,1:T(8,128)S(1)} %convolution_subtract_fusion, f32[64,64]{1,0:T(8,128)S(1)} %get-tuple-element.31, f32[64,64]{1,0:T(8,128)S(1)} %get-tuple-element.32), kind=kOutput, calls=%fused_computation.32 | convolution fusion | flops 202694656 | bytes 4227072 | tf_op jit(solution)/shard_map/dot_general | solution.py:76
  (95 shorter events, 98.5 us)
Async XLA Ops:
  0.0 21.4 %copy-start.7 = (f32[1,1,2,2,32,3072]{5,4,3,2,1,0:T(8,128)S(1)}, f32[1,1,2,2,32,3072]{5,4,3,2,1,0:T(8,128)}, u32[]{:S(2)}) copy-start(f32[1,1,2,2,32,3072]{5,4,3,2,1,0:T(8,128)} %param.2) | copy-start | bytes 4718596
  0.0 95.2 %collective-permute-start.1 = (f32[1,256,128]{2,1,0:T(8,128)}, f32[1,256,128]{2,1,0:T(8,128)S(1)}, u32[]{:S(2)}, u32[]{:S(2)}) collective-permute-start(f32[1,256,128]{2,1,0:T(8,128)} %param.3), channel_id=1, source_target_pairs={{1,0},{2,1},{3,2},{0,3},{5,4},{6,5},{7,6},{4,7},{9,8},{10,9},{11,1... | collective-permute-start | bytes 393224 | tf_op jit(solution)/shard_map/ppermute | solution.py:19
  0.4 95.5 %collective-permute-start.2 = (f32[1,256,128]{2,1,0:T(8,128)}, f32[1,256,128]{2,1,0:T(8,128)S(1)}, u32[]{:S(2)}, u32[]{:S(2)}) collective-permute-start(f32[1,256,128]{2,1,0:T(8,128)} %param.3), channel_id=1, source_target_pairs={{2,0},{3,1},{0,2},{1,3},{6,4},{7,5},{4,6},{5,7},{10,8},{11,9},{8,1... | collective-permute-start | bytes 393224 | tf_op jit(solution)/shard_map/ppermute | solution.py:19
  3.0 93.5 %collective-permute-start.3 = (f32[1,256,128]{2,1,0:T(8,128)}, f32[1,256,128]{2,1,0:T(8,128)}, u32[]{:S(2)}, u32[]{:S(2)}) collective-permute-start(f32[1,256,128]{2,1,0:T(8,128)} %param.3), channel_id=1, source_target_pairs={{3,0},{0,1},{1,2},{2,3},{7,4},{4,5},{5,6},{6,7},{11,8},{8,9},{9,10... | collective-permute-start | bytes 393224 | tf_op jit(solution)/shard_map/ppermute | solution.py:19
  6.0 15.4 %collective-permute-start = (f32[1,2,2,32,1024]{4,3,2,1,0:T(8,128)S(1)}, f32[1,2,2,32,1024]{4,3,2,1,0:T(8,128)}, u32[]{:S(2)}, u32[]{:S(2)}) collective-permute-start(f32[1,2,2,32,1024]{4,3,2,1,0:T(8,128)S(1)} %slice.32), channel_id=1, source_target_pairs={{0,1},{1,2},{2,3},{4,5},{5,6},{6,7},{8,9},{9,10},{10,11},{12,13},{... | collective-permute-start | bytes 1572872 | tf_op jit(solution)/shard_map/ppermute | solution.py:11
  35.0 4.4 %copy-start.2 = (f32[2,32,64,64]{3,2,1,0:T(8,128)S(1)}, f32[2,32,64,64]{3,2,1,0:T(8,128)}, u32[]{:S(2)}) copy-start(f32[2,32,64,64]{3,2,1,0:T(8,128)} %reshape.540) | copy-start | bytes 3145732
  35.0 4.4 %copy-start.4 = (f32[64,2,32,64]{3,0,2,1:T(8,128)S(1)}, f32[64,2,32,64]{3,0,2,1:T(8,128)}, u32[]{:S(2)}) copy-start(f32[64,2,32,64]{3,0,2,1:T(8,128)} %fusion.96) | copy-start | bytes 3145732
  41.5 5.6 %copy-start = (f32[64,2,32,64]{3,0,2,1:T(8,128)}, f32[64,2,32,64]{3,0,2,1:T(8,128)S(1)}, u32[]{:S(2)}) copy-start(f32[64,2,32,64]{3,0,2,1:T(8,128)S(1)} %convolution_add_fusion.1) | copy-start | bytes 3145732
  85.8 8.5 %copy-start.10 = (f32[1,256,128]{2,1,0:T(8,128)S(1)}, f32[1,256,128]{2,1,0:T(8,128)}, u32[]{:S(2)}) copy-start(f32[1,256,128]{2,1,0:T(8,128)} %param.3) | copy-start | bytes 393220
  85.8 38.5 %all-to-all-start = ((f32[32,1,16384]{2,1,0:T(1,128)}), f32[32,1,16384]{2,1,0:T(1,128)S(1)}, u32[]{:S(2)}, u32[]{:S(2)}) async-start(f32[32,1,16384]{2,1,0:T(1,128)} %reshape.578), calls=%async_computation | async-start | bytes 4194304 | tf_op jit(solution)/shard_map/all_to_all | solution.py:126
  124.3 1.3 copy-start.6
  179.3 2.4 copy-start.8
  179.3 2.4 copy-start.9
  185.0 34.0 %all-to-all-start.1 = ((f32[1,2,2,1024,128]{4,1,2,0,3:T(2,128)}), f32[1,2,2,1024,128]{4,1,2,0,3:T(2,128)S(1)}, u32[]{:S(2)}, u32[]{:S(2)}) async-start(f32[1,2,2,1024,128]{4,1,2,0,3:T(2,128)} %copy.140), calls=%async_computation.1 | async-start | bytes 4194304 | tf_op jit(solution)/shard_map/all_to_all | solution.py:145
  238.1 4.4 %copy-start.3 = (f32[2,32,64,64]{3,2,1,0:T(8,128)S(1)}, f32[2,32,64,64]{3,2,1,0:T(8,128)}, u32[]{:S(2)}) copy-start(f32[2,32,64,64]{3,2,1,0:T(8,128)} %reshape.557) | copy-start | bytes 3145732
  238.1 4.4 %copy-start.5 = (f32[64,2,32,64]{3,0,2,1:T(8,128)S(1)}, f32[64,2,32,64]{3,0,2,1:T(8,128)}, u32[]{:S(2)}) copy-start(f32[64,2,32,64]{3,0,2,1:T(8,128)} %fusion.86) | copy-start | bytes 3145732
  244.6 5.6 %copy-start.1 = (f32[64,2,32,64]{3,0,2,1:T(8,128)}, f32[64,2,32,64]{3,0,2,1:T(8,128)S(1)}, u32[]{:S(2)}) copy-start(f32[64,2,32,64]{3,0,2,1:T(8,128)S(1)} %convolution_add_fusion) | copy-start | bytes 3145732
where the time goes:
time: 275 us; the launch traced here: 270 us
  local copies, waits for them, and re-layouts  93.1 us (34%)
  matrix products  81.4 us (30%)
  waiting for transfers between devices  56.1 us (20%)
  other arithmetic  19.8 us (7%)
  starting transfers between devices  19.4 us (7%)
    all_to_all x1, waiting for transfers between devices, per_device(): lax.all_to_all(columns, 'band', split_axis=3, concat_axis=4, tiled=True)  29.8 us
    unnamed x31, local copies, waits for them, and re-layouts  26.3 us
    all_to_all x1, waiting for transfers between devices, per_device(): lax.all_to_all(stacked, 'band', split_axis=4, concat_axis=3, tiled=True)  19.2 us
    dot_general x4, matrix products, transform_last(): jnp.matmul(first_real, sin_inner, precision=highest)  14.5 us
    all_to_all x3, local copies, waits for them, and re-layouts, per_device(): lax.all_to_all(stacked, 'band', split_axis=4, concat_axis=3, tiled=True)  12.6 us
    dot_general x4, matrix products, transform_last(): jnp.einsum('...nj,nk->...kj', imag_part, sin_outer, precision=highest)  11.3 us
    dot_general x4, matrix products, transform_last(): jnp.matmul(first_imag, cos_inner, precision=highest)  10.5 us
    dot_general x4, matrix products, transform_last(): jnp.einsum('...nj,nk->...kj', real_part, cos_outer, precision=highest)  10.5 us
  transfers between devices with their start and end apart: 6, of which 3 were waited for; matrix products, arithmetic and copies ran while one was open for 31% of the time, Pallas kernels for 0%

commit v1 on v0

--- a/solution.py
+++ b/solution.py
@@ -123,7 +123,14 @@
         -2.0 * math.pi / length,
     )
     stacked = jnp.stack([real_part, imag_part], axis=2)
-    spectra = row_pass(lax.all_to_all(stacked, "band", split_axis=4, concat_axis=3, tiled=True))
+    spectra = row_pass(
+        jnp.concatenate(
+            lax.all_to_all(
+                jnp.stack(jnp.split(stacked, lax.axis_size("band"), axis=4)), "band", 0, 0
+            ),
+            axis=3,
+        )
+    )
     real_part, imag_part = (spectra[:, :, 0], spectra[:, :, 1])
     phases = gathered(chirp_phase, "seg", 1)
     cosine = jnp.cos(phases)[:, None]

time: 275 us -> 246 us (0.89)
  local copies, waits for them, and re-layouts: 93.1 us -> 51.8 us
  other arithmetic: 19.8 us -> 32.5 us
    unnamed x31 -> x27, local copies, waits for them, and re-layouts: 26.3 us -> 5.6 us
    unnamed x0 -> x31, other arithmetic: none -> 19.7 us
    all_to_all x3 -> x0, local copies, waits for them, and re-layouts: 12.6 us -> none  [per_device(): lax.all_to_all(stacked, 'band', split_axis=4, concat_axis=3, tiled=True)]
    another operation x4 -> x3, local copies, waits for them, and re-layouts: 15.5 us -> 6.93 us  [the longest x1 8.36 us: per_device(): stacked = jnp.stack([real_part, imag_part], axis=2)]
    all_to_all x1 -> x0, other arithmetic: 7.39 us -> none  [per_device(): lax.all_to_all(stacked, 'band', split_axis=4, concat_axis=3, tiled=True)]
  transfers between devices with their start and end apart: 6 -> 6, of which waited for: 3 -> 3; matrix products, arithmetic and copies ran while one was open for 31% -> 35% of each run, Pallas kernels for 0% -> 0%
where the time goes in v1:
time: 246 us; the launch traced here: 242 us
  matrix products  81.7 us (33%)
  waiting for transfers between devices  55.9 us (23%)
  local copies, waits for them, and re-layouts  51.8 us (21%)
  other arithmetic  32.5 us (13%)
  starting transfers between devices  19.2 us (8%)
    all_to_all x1, waiting for transfers between devices, per_device(): lax.all_to_all(columns, 'band', split_axis=3, concat_axis=4, tiled=True)  29.8 us
    unnamed x31, other arithmetic  19.7 us
    all_to_all x1, waiting for transfers between devices, per_device(): lax.all_to_all(jnp.stack(jnp.split(stacked, lax.axis_size('band'), axis=4...  19 us
    dot_general x4, matrix products, transform_last(): jnp.matmul(first_real, sin_inner, precision=highest)  14.4 us
    dot_general x4, matrix products, transform_last(): jnp.einsum('...nj,nk->...kj', imag_part, sin_outer, precision=highest)  11.3 us
    dot_general x4, matrix products, transform_last(): jnp.matmul(first_imag, cos_inner, precision=highest)  10.6 us
    dot_general x4, matrix products, transform_last(): jnp.einsum('...nj,nk->...kj', real_part, cos_outer, precision=highest)  10.4 us
    dot_general x4, matrix products, transform_last(): jnp.matmul(first_real, cos_inner, precision=highest)  10.2 us
  transfers between devices with their start and end apart: 6, of which 3 were waited for; matrix products, arithmetic and copies ran while one was open for 35% of the time, Pallas kernels for 0%

profile of v1, /device:TPU:8, one launch (start us, length us, event | category | flops | bytes accessed | tf_op | source)
XLA Modules:
  0.0 241.9 jit_solution(8297500860540753426)
XLA Ops:
  8.0 3.3 %fusion.81 = (f32[32,4096]{1,0:T(8,128)}, f32[32,4096]{1,0:T(8,128)}) fusion(s32[32]{0:T(128)S(1)} %iota_add_fusion.1), kind=kLoop, calls=%fused_computation.178 | loop fusion | flops 1835008 | bytes 1048704 | tf_op jit(solution)/shard_map/cos | solution.py:44
  11.4 2.9 %fusion.79 = (f32[1024,128]{1,0:T(8,128)}, f32[1024,128]{1,0:T(8,128)}) fusion(s32[128]{0:T(128)S(1)} %iota_add_fusion), kind=kLoop, calls=%fused_computation.176 | loop fusion | flops 1835008 | bytes 1049088 | tf_op jit(solution)/shard_map/cos | solution.py:44
  14.3 7.1 %collective-permute-done = f32[1,2,2,32,1024]{4,3,2,1,0:T(8,128)} collective-permute-done((f32[1,2,2,32,1024]{4,3,2,1,0:T(8,128)S(1)}, f32[1,2,2,32,1024]{4,3,2,1,0:T(8,128)}, u32[]{:S(2)}, u32[]{:S(2)}) %collective-permute-start) | collective-permute-done | bytes 524320 | tf_op jit(solution)/shard_map/ppermute | solution.py:11
  26.1 3.3 %fusion.124 = f32[64,2,32,64]{3,0,2,1:T(8,128)} fusion(f32[2,32,64,64]{3,2,1,0:T(8,128)S(1)} %reshape.547), kind=kOutput, calls=%fused_computation.267 | convolution fusion | flops 201383936 | bytes 2097152 | tf_op jit(solution)/shard_map/...nj,nk->...kj/dot_general | solution.py:60
  29.4 3.4 %fusion.128 = f32[64,2,32,64]{3,0,2,1:T(8,128)} fusion(f32[2,32,64,64]{3,2,1,0:T(8,128)S(1)} %reshape.547), kind=kOutput, calls=%fused_computation.271 | convolution fusion | flops 201383936 | bytes 2097152 | tf_op jit(solution)/shard_map/...nj,nk->...kj/dot_general | solution.py:63
  35.0 4.4 %convolution_subtract_fusion.1 = f32[64,2,32,64]{3,0,2,1:T(8,128)S(1)} fusion(f32[64,2,32,64]{3,0,2,1:T(8,128)} %fusion.124, f32[2,32,64,64]{3,2,1,0:T(8,128)} %reshape.546), kind=kOutput, calls=%fused_computation.100 | convolution fusion | flops 201646080 | bytes 3145728 | tf_op jit(solution)/shard_map/...nj,nk->...kj/dot_general | solution.py:58
  43.6 3.5 %fusion.10 = f32[2,32,64,64]{3,2,1,0:T(8,128)} fusion(f32[64,2,32,64]{3,0,2,1:T(8,128)S(1)} %convolution_add_fusion.1, f32[64,2,32,64]{3,0,2,1:T(8,128)S(1)} %convolution_subtract_fusion.1, f32[64,64]{1,0:T(8,128)S(1)} %get-tuple-element.25, f32[64,64]{1,0:T(8,128)S(1)} %get-tuple-element.26), kind=kOutput, calls=%fused_computation.79 | convolution fusion | flops 202170368 | bytes 3178496 | tf_op jit(solution)/shard_map/dot_general | solution.py:76
  47.1 3.4 %subtract_bitcast_fusion = f32[1,2,32,64,64]{3,4,2,1,0:T(8,128)} fusion(f32[2,32,64,64]{3,2,1,0:T(8,128)S(1)} %fusion.12, f32[64,2,32,64]{3,0,2,1:T(8,128)S(1)} %convolution_add_fusion.1, f32[64,2,32,64]{3,0,2,1:T(8,128)S(1)} %convolution_subtract_fusion.1, f32[64,64]{1,0:T(8,128)S(1)} %get-tuple-element.25, f32[64,64]{1,0:T(8,128)S(1)} %get-tuple-element.26), kind=kOutput, calls=%fused_computation.96 | convolution fusion | flops 202432512 | bytes 4227072 | tf_op jit(solution)/shard_map/dot_general | solution.py:73
  50.5 3.0 %copy.86 = f32[1,2,32,64,64]{4,3,2,1,0:T(8,128)} copy(f32[1,2,32,64,64]{3,4,2,1,0:T(8,128)} %subtract_bitcast_fusion) | data formatting | bytes 2097152 | tf_op jit(solution)/shard_map/transpose | solution.py:79
  55.6 5.5 %add_bitcast_fusion = f32[1,2,32,64,64]{3,4,2,1,0:T(8,128)} fusion(f32[2,32,64,64]{3,2,1,0:T(8,128)} %fusion.10, f32[64,2,32,64]{3,0,2,1:T(8,128)} %copy-done, f32[64,2,32,64]{3,0,2,1:T(8,128)S(1)} %convolution_subtract_fusion.1, f32[64,64]{1,0:T(8,128)S(1)} %get-tuple-element.25, f32[64,64]{1,0:T(8,128)S(1)} %get-tuple-element.26), kind=kOutput, calls=%fused_computation.95 | convolution fusion | flops 202432512 | bytes 4227072 | tf_op jit(solution)/shard_map/dot_general | solution.py:76
  86.8 8.3 %all-to-all-start = ((f32[32,1,2,2,32,128]{5,4,2,3,1,0:T(8,128)}), f32[32,1,2,2,32,128]{5,4,2,3,1,0:T(8,128)S(1)}, u32[]{:S(2)}, u32[]{:S(2)}) async-start(f32[32,1,2,2,32,128]{5,4,2,3,1,0:T(8,128)} %constant_dynamic-update-slice_fusion), calls=%async_computation | async-start | bytes 4194304 | tf_op jit(solution)/shard_map/all_to_all | solution.py:128
  102.5 3.0 %dynamic-slice_cosine_fusion = (f32[4,1,256,128]{3,2,1,0:T(8,128)S(1)}, f32[4,1,256,128]{3,2,1,0:T(8,128)S(1)}) fusion(f32[8,1,256,128]{3,2,1,0:T(8,128)} %bitcast_dynamic-update-slice_fusion.1, s32[]{:T(128)S(6)} %select_n.195), kind=kLoop, calls=%fused_computation.174 | loop fusion | bytes 1572868 | tf_op jit(solution)/shard_map/cos | solution.py:136
  106.1 19.0 %all-to-all-done = f32[32,1,2,2,32,128]{5,4,2,3,1,0:T(8,128)S(1)} async-done(((f32[32,1,2,2,32,128]{5,4,2,3,1,0:T(8,128)}), f32[32,1,2,2,32,128]{5,4,2,3,1,0:T(8,128)S(1)}, u32[]{:S(2)}, u32[]{:S(2)}) %all-to-all-start) | async-done | bytes 2097184 | tf_op jit(solution)/shard_map/all_to_all | solution.py:128
  153.5 2.9 %copy.105 = f32[1,2,2,1024,128]{4,1,2,0,3:T(2,128)} copy(f32[1,2,2,1024,128]{4,3,1,2,0:T(8,128)S(1)} %pad_maximum_fusion) | data formatting | bytes 4194304 | tf_op jit(solution)/shard_map/stack | solution.py:151
  156.4 4.0 %all-to-all-start.1 = ((f32[1,2,2,1024,128]{4,1,2,0,3:T(2,128)}), f32[1,2,2,1024,128]{4,1,2,0,3:T(2,128)S(1)}, u32[]{:S(2)}, u32[]{:S(2)}) async-start(f32[1,2,2,1024,128]{4,1,2,0,3:T(2,128)} %copy.105), calls=%async_computation.1 | async-start | bytes 4194304 | tf_op jit(solution)/shard_map/all_to_all | solution.py:152
  160.6 29.8 %all-to-all-done.1 = f32[1,2,2,1024,128]{4,1,2,0,3:T(2,128)S(1)} async-done(((f32[1,2,2,1024,128]{4,1,2,0,3:T(2,128)}), f32[1,2,2,1024,128]{4,1,2,0,3:T(2,128)S(1)}, u32[]{:S(2)}, u32[]{:S(2)}) %all-to-all-start.1) | async-done | bytes 2097184 | tf_op jit(solution)/shard_map/all_to_all | solution.py:152
  191.8 6.4 %slice_reduce_fusion = (f32[2,32,4096]{2,1,0:T(8,128)S(1)}, f32[2,32,4096]{2,1,0:T(8,128)}) fusion(f32[1,2,2,32,4096]{4,0,3,2,1:T(1,128)S(1)} %bitcast.429), kind=kLoop, calls=%fused_computation.120 | loop fusion | bytes 4194304 | tf_op jit(solution)/shard_map/slice | solution.py:99
  200.4 3.3 %fusion.134 = f32[64,2,32,64]{3,0,2,1:T(8,128)} fusion(f32[2,32,64,64]{3,2,1,0:T(8,128)S(1)} %reshape.564), kind=kOutput, calls=%fused_computation.277 | convolution fusion | flops 201383936 | bytes 2097152 | tf_op jit(solution)/shard_map/...nj,nk->...kj/dot_general | solution.py:58
  203.8 3.4 %fusion.118 = f32[64,2,32,64]{3,0,2,1:T(8,128)} fusion(f32[2,32,64,64]{3,2,1,0:T(8,128)S(1)} %reshape.564), kind=kOutput, calls=%fused_computation.261 | convolution fusion | flops 201383936 | bytes 2097152 | tf_op jit(solution)/shard_map/...nj,nk->...kj/dot_general | solution.py:61
  209.3 4.4 %convolution_subtract_fusion = f32[64,2,32,64]{3,0,2,1:T(8,128)S(1)} fusion(f32[64,2,32,64]{3,0,2,1:T(8,128)} %fusion.134, f32[2,32,64,64]{3,2,1,0:T(8,128)} %reshape.565), kind=kOutput, calls=%fused_computation.98 | convolution fusion | flops 201646080 | bytes 3145728 | tf_op jit(solution)/shard_map/...nj,nk->...kj/dot_general | solution.py:60
  218.0 3.6 %fusion = f32[2,32,64,64]{3,2,1,0:T(8,128)} fusion(f32[64,2,32,64]{3,0,2,1:T(8,128)S(1)} %convolution_add_fusion, f32[64,2,32,64]{3,0,2,1:T(8,128)S(1)} %convolution_subtract_fusion, f32[64,64]{1,0:T(8,128)S(1)} %get-tuple-element.31, f32[64,64]{1,0:T(8,128)S(1)} %get-tuple-element.32), kind=kOutput, calls=%fused_computation.65 | convolution fusion | flops 202170368 | bytes 3178496 | tf_op jit(solution)/shard_map/dot_general | solution.py:76
  221.5 3.4 %multiply_bitcast_fusion.1 = f32[1,2,32,64,64]{3,4,2,1,0:T(8,128)} fusion(f32[2,32,64,64]{3,2,1,0:T(8,128)S(1)} %fusion.2, f32[64,2,32,64]{3,0,2,1:T(8,128)S(1)} %convolution_add_fusion, f32[64,2,32,64]{3,0,2,1:T(8,128)S(1)} %convolution_subtract_fusion, f32[64,64]{1,0:T(8,128)S(1)} %get-tuple-element.31, f32[64,64]{1,0:T(8,128)S(1)} %get-tuple-element.32), kind=kOutput, calls=%fused_computation.94 | convolution fusion | flops 202694656 | bytes 4227072 | tf_op jit(solution)/shard_map/dot_general | solution.py:73
  224.9 3.0 %copy.112 = f32[1,2,32,64,64]{4,3,2,1,0:T(8,128)} copy(f32[1,2,32,64,64]{3,4,2,1,0:T(8,128)} %multiply_bitcast_fusion.1) | data formatting | bytes 2097152 | tf_op jit(solution)/shard_map/mul | solution.py:100
  230.1 5.5 %multiply_bitcast_fusion = f32[1,2,32,64,64]{3,4,2,1,0:T(8,128)} fusion(f32[2,32,64,64]{3,2,1,0:T(8,128)} %fusion, f32[64,2,32,64]{3,0,2,1:T(8,128)} %copy-done.1, f32[64,2,32,64]{3,0,2,1:T(8,128)S(1)} %convolution_subtract_fusion, f32[64,64]{1,0:T(8,128)S(1)} %get-tuple-element.31, f32[64,64]{1,0:T(8,128)S(1)} %get-tuple-element.32), kind=kOutput, calls=%fused_computation.93 | convolution fusion | flops 202694656 | bytes 4227072 | tf_op jit(solution)/shard_map/dot_general | solution.py:76
  (118 shorter events, 101.3 us)
Async XLA Ops:
  0.0 21.4 %copy-start.6 = (f32[1,1,2,2,32,3072]{5,4,3,2,1,0:T(8,128)S(1)}, f32[1,1,2,2,32,3072]{5,4,3,2,1,0:T(8,128)}, u32[]{:S(2)}) copy-start(f32[1,1,2,2,32,3072]{5,4,3,2,1,0:T(8,128)} %param.2) | copy-start | bytes 4718596
  0.0 96.0 %collective-permute-start.1 = (f32[1,256,128]{2,1,0:T(8,128)}, f32[1,256,128]{2,1,0:T(8,128)S(1)}, u32[]{:S(2)}, u32[]{:S(2)}) collective-permute-start(f32[1,256,128]{2,1,0:T(8,128)} %param.3), channel_id=1, source_target_pairs={{1,0},{2,1},{3,2},{0,3},{5,4},{6,5},{7,6},{4,7},{9,8},{10,9},{11,1... | collective-permute-start | bytes 393224 | tf_op jit(solution)/shard_map/ppermute | solution.py:19
  0.4 96.3 %collective-permute-start.2 = (f32[1,256,128]{2,1,0:T(8,128)}, f32[1,256,128]{2,1,0:T(8,128)S(1)}, u32[]{:S(2)}, u32[]{:S(2)}) collective-permute-start(f32[1,256,128]{2,1,0:T(8,128)} %param.3), channel_id=1, source_target_pairs={{2,0},{3,1},{0,2},{1,3},{6,4},{7,5},{4,6},{5,7},{10,8},{11,9},{8,1... | collective-permute-start | bytes 393224 | tf_op jit(solution)/shard_map/ppermute | solution.py:19
  3.0 94.3 %collective-permute-start.3 = (f32[1,256,128]{2,1,0:T(8,128)}, f32[1,256,128]{2,1,0:T(8,128)}, u32[]{:S(2)}, u32[]{:S(2)}) collective-permute-start(f32[1,256,128]{2,1,0:T(8,128)} %param.3), channel_id=1, source_target_pairs={{3,0},{0,1},{1,2},{2,3},{7,4},{4,5},{5,6},{6,7},{11,8},{8,9},{9,10... | collective-permute-start | bytes 393224 | tf_op jit(solution)/shard_map/ppermute | solution.py:19
  6.0 15.4 %collective-permute-start = (f32[1,2,2,32,1024]{4,3,2,1,0:T(8,128)S(1)}, f32[1,2,2,32,1024]{4,3,2,1,0:T(8,128)}, u32[]{:S(2)}, u32[]{:S(2)}) collective-permute-start(f32[1,2,2,32,1024]{4,3,2,1,0:T(8,128)S(1)} %slice.32), channel_id=1, source_target_pairs={{0,1},{1,2},{2,3},{4,5},{5,6},{6,7},{8,9},{9,10},{10,11},{12,13},{... | collective-permute-start | bytes 1572872 | tf_op jit(solution)/shard_map/ppermute | solution.py:11
  35.0 4.4 %copy-start.2 = (f32[2,32,64,64]{3,2,1,0:T(8,128)S(1)}, f32[2,32,64,64]{3,2,1,0:T(8,128)}, u32[]{:S(2)}) copy-start(f32[2,32,64,64]{3,2,1,0:T(8,128)} %reshape.546) | copy-start | bytes 3145732
  35.0 4.4 %copy-start.4 = (f32[64,2,32,64]{3,0,2,1:T(8,128)S(1)}, f32[64,2,32,64]{3,0,2,1:T(8,128)}, u32[]{:S(2)}) copy-start(f32[64,2,32,64]{3,0,2,1:T(8,128)} %fusion.128) | copy-start | bytes 3145732
  41.5 5.6 %copy-start = (f32[64,2,32,64]{3,0,2,1:T(8,128)}, f32[64,2,32,64]{3,0,2,1:T(8,128)S(1)}, u32[]{:S(2)}) copy-start(f32[64,2,32,64]{3,0,2,1:T(8,128)S(1)} %convolution_add_fusion.1) | copy-start | bytes 3145732
  86.8 8.3 %copy-start.9 = (f32[1,256,128]{2,1,0:T(8,128)S(1)}, f32[1,256,128]{2,1,0:T(8,128)}, u32[]{:S(2)}) copy-start(f32[1,256,128]{2,1,0:T(8,128)} %param.3) | copy-start | bytes 393220
  86.8 38.3 %all-to-all-start = ((f32[32,1,2,2,32,128]{5,4,2,3,1,0:T(8,128)}), f32[32,1,2,2,32,128]{5,4,2,3,1,0:T(8,128)S(1)}, u32[]{:S(2)}, u32[]{:S(2)}) async-start(f32[32,1,2,2,32,128]{5,4,2,3,1,0:T(8,128)} %constant_dynamic-update-slice_fusion), calls=%async_computation | async-start | bytes 4194304 | tf_op jit(solution)/shard_map/all_to_all | solution.py:128
  150.7 2.4 copy-start.7
  150.8 2.4 copy-start.8
  156.4 34.0 %all-to-all-start.1 = ((f32[1,2,2,1024,128]{4,1,2,0,3:T(2,128)}), f32[1,2,2,1024,128]{4,1,2,0,3:T(2,128)S(1)}, u32[]{:S(2)}, u32[]{:S(2)}) async-start(f32[1,2,2,1024,128]{4,1,2,0,3:T(2,128)} %copy.105), calls=%async_computation.1 | async-start | bytes 4194304 | tf_op jit(solution)/shard_map/all_to_all | solution.py:152
  209.3 4.4 %copy-start.3 = (f32[2,32,64,64]{3,2,1,0:T(8,128)S(1)}, f32[2,32,64,64]{3,2,1,0:T(8,128)}, u32[]{:S(2)}) copy-start(f32[2,32,64,64]{3,2,1,0:T(8,128)} %reshape.565) | copy-start | bytes 3145732
  209.3 4.4 %copy-start.5 = (f32[64,2,32,64]{3,0,2,1:T(8,128)S(1)}, f32[64,2,32,64]{3,0,2,1:T(8,128)}, u32[]{:S(2)}) copy-start(f32[64,2,32,64]{3,0,2,1:T(8,128)} %fusion.118) | copy-start | bytes 3145732
  215.8 5.7 %copy-start.1 = (f32[64,2,32,64]{3,0,2,1:T(8,128)}, f32[64,2,32,64]{3,0,2,1:T(8,128)S(1)}, u32[]{:S(2)}) copy-start(f32[64,2,32,64]{3,0,2,1:T(8,128)S(1)} %convolution_add_fusion) | copy-start | bytes 3145732
